TPU v7x, 128 devices: a whole 4x4x4 slice. The times are simulated.
128 devices in a mesh: row: 8 (over y, core), col: 16 (over z, x).
Axes of the slice: x: 4, y: 4, z: 4, core: 2. Of those that a mesh axis runs over, the one named last changes fastest.
Arguments:
- mock_maps: bfloat16 [1024, 163840], P('col', 'row'), may hold values from -6 to 6
- window_blocks: int32 [4], replicated, may hold values from 0 to 127, as said below
- kept_tiles: int32 [128, 4], P(('row', 'col')), may hold values from 0 to 1, as said below
- taper_index: int32 [128, 4], P(('row', 'col')), may hold values from 0 to 3, as said below
- taper_table: float32 [4], replicated, may hold values from 0.25 to 2
Outputs:
- covariance: bfloat16 [163840, 5120], P(('row', 'col'))
Inputs may be any that keep to these rules, and one draw needn't show every extreme that they name: `window_blocks`: the entries are distinct feature blocks; the first and the last feature block are always among them. `kept_tiles`: A tile whose row block is its own window column block is always kept. `taper_index`: A tile whose row block is its own window column block takes entry 0.
All inputs are finite; a program needn't handle non-finite values.
Results may differ from a plain program's by a relative error of at most 0.001.
Values may be sent and summed in bfloat16 or wider, within the bound.
No kernel may reach another device: no remote copies, remote signals or barrier semaphores. Data moves between devices by JAX's collectives and lax.ppermute only.
A program may use at most 128 MiB of HBM per device.

v0:
```python
import jax
import jax.numpy as jnp
from jax import lax
from jax.sharding import PartitionSpec as P

WINDOW = 4


def per_device(mock_maps, window_blocks, kept_tiles, taper_index, taper_table):
    block_width = mock_maps.shape[1] // lax.axis_size("col")
    local_blocks = mock_maps.shape[1] // block_width
    row = lax.axis_index("row")
    chunks = []
    for slot in range(WINDOW):
        local_id = window_blocks[slot] - row * local_blocks
        mine = (local_id >= 0) & (local_id < local_blocks)
        start = jnp.clip(local_id, 0, local_blocks - 1) * block_width
        piece = lax.dynamic_slice_in_dim(mock_maps, start, block_width, 1)
        chunks.append(jnp.where(mine, piece, jnp.zeros_like(piece)))
    local_panels = lax.psum(jnp.concatenate(chunks, axis=1), "row")
    panels = lax.all_gather(local_panels, "col", axis=0, tiled=True)
    own_block = lax.all_to_all(mock_maps, "col", split_axis=1, concat_axis=0, tiled=True)
    mock_count = own_block.shape[0]
    own_mean = jnp.sum(own_block, axis=0, dtype=jnp.float32) / mock_count
    panel_mean = jnp.sum(panels, axis=0, dtype=jnp.float32) / mock_count
    products = lax.dot_general(
        own_block, panels, (((0,), (0,)), ((), ())), preferred_element_type=jnp.float32
    )
    classes = jnp.arange(taper_table.shape[0], dtype=jnp.int32)
    weights = jnp.sum(
        jnp.where(
            classes[None, :] == taper_index[0][:, None], taper_table[None, :], jnp.float32(0.0)
        ),
        axis=1,
    )
    weight_cols = jnp.repeat(weights, block_width)
    keep_cols = jnp.repeat(kept_tiles[0], block_width)
    centred = products - mock_count * own_mean[:, None] * panel_mean[None, :]
    tile_value = weight_cols[None, :] * centred / (mock_count - 1)
    tile_value = jnp.where(keep_cols[None, :] > 0, tile_value, jnp.float32(0.0))
    return tile_value.astype(jnp.bfloat16)


def solution(mesh):
    in_specs = (P("col", "row"), P(), P(("row", "col"), None), P(("row", "col"), None), P())
    out_specs = P(("row", "col"), None)
    return jax.shard_map(
        per_device, mesh=mesh, in_specs=in_specs, out_specs=out_specs, check_vma=False
    )
```

profile of v0, /device:TPU:1, one launch (start us, length us, event | category | flops | bytes accessed | tf_op | source)
XLA Modules:
  0.0 236.2 jit_solution(14619275543654786151)
XLA Ops:
  6.5 0.0 copy-start.2
  6.5 0.0 copy-start.3
  6.5 0.0 copy-start.4
  6.5 0.0 all-reduce.2.cloned.1.call-start
  6.5 1.4 fusion.4
  10.4 1.3 dynamic-slice_select_fusion.3
  11.7 0.9 pad_maximum_fusion
  12.6 0.0 all-reduce.2.cloned.1.call-update
  12.6 0.0 all-gather.2.cloned.1.call-start
  12.7 62.7 %all-reduce.2.cloned.1.call-done = bf16[64,5120]{1,0:T(8,128)(2,1)} async-done(((bf16[64,5120]{1,0:T(8,128)(2,1)}), bf16[64,5120]{1,0:T(8,128)(2,1)}) %all-reduce.2.cloned.1.call-update) | async-done | bytes 655376 | tf_op jit(solution)/shard_map/psum | solution.py:20
  75.4 0.0 all-gather.2.cloned.1.call-update
  75.4 3.5 %copy.16 = bf16[8,16,8,1280]{3,2,0,1:T(8,128)(2,1)} copy(bf16[8,16,8,1280]{3,2,1,0:T(8,128)(2,1)} %bitcast.29) | data formatting | bytes 5242880 | tf_op jit(solution)/shard_map/all_to_all | solution.py:22
  78.9 6.7 %all-to-all-start = ((bf16[64,16,1280]{2,0,1:T(8,128)(2,1)}), bf16[64,16,1280]{2,0,1:T(8,128)(2,1)S(1)}, u32[]{:S(2)}, u32[]{:S(2)}) async-start(bf16[64,16,1280]{2,0,1:T(8,128)(2,1)} %bitcast.28), calls=%async_computation | async-start | bytes 5242880 | tf_op jit(solution)/shard_map/all_to_all | solution.py:22
  85.6 0.0 copy-done.2
  85.6 0.1 broadcast_in_dim.34
  85.7 0.0 copy-done.3
  85.7 0.0 copy-done.4
  85.7 0.2 select_reduce_fusion
  85.9 0.1 broadcast_in_dim.38
  86.0 39.3 %all-to-all-done = bf16[64,16,1280]{2,0,1:T(8,128)(2,1)S(1)} async-done(((bf16[64,16,1280]{2,0,1:T(8,128)(2,1)}), bf16[64,16,1280]{2,0,1:T(8,128)(2,1)S(1)}, u32[]{:S(2)}, u32[]{:S(2)}) %all-to-all-start) | async-done | bytes 2621472 | tf_op jit(solution)/shard_map/all_to_all | solution.py:22
  125.3 0.0 copy-start.1
  125.3 0.4 convert_reduce_fusion.1
  125.8 1.1 copy-done.1
  126.8 57.5 %all-gather.2.cloned.1.call-done = bf16[1024,5120]{1,0:T(8,128)(2,1)} async-done(((bf16[64,5120]{1,0:T(8,128)(2,1)}), bf16[1024,5120]{1,0:T(8,128)(2,1)}) %all-gather.2.cloned.1.call-update) | async-done | bytes 10485776 | tf_op jit(solution)/shard_map/all_gather | solution.py:21
  184.3 0.0 copy-start
  184.3 5.6 %convert_reduce_fusion = f32[5120]{0:T(1024)S(1)} fusion(bf16[1024,5120]{1,0:T(8,128)(2,1)} %all-gather.2.cloned.1.call-done), kind=kLoop, calls=%fused_computation.5 | loop fusion | flops 10480640 | bytes 10506240 | tf_op jit(solution)/shard_map/reduce_sum | solution.py:25
  189.9 1.3 copy-done
  191.3 20.5 %fusion.3 = bf16[1280,5120]{0,1:T(8,128)(2,1)} fusion(bf16[1024,5120]{1,0:T(8,128)(2,1)S(1)} %copy-done, bf16[1024,1280]{1,0:T(8,128)(2,1)} %bitcast.27, f32[5120]{0:T(1024)S(1)} %broadcast_multiply_fusion, f32[1280]{0:T(1024)S(1)} %convert_reduce_fusion.1, f32[5120]{0:T(1024)S(1)} %mul.45, pred[5120]{0:T(1024)(128)(4,1)S(1)} %gt.21), kind=kOutput, calls=%fused_computation.4 | convolution fusion | flops 13461094400 | bytes 26265600 | tf_op jit(solution)/shard_map/dot_general | solution.py:26
  211.7 17.6 %copy.13 = bf16[1280,5120]{1,0:T(8,128)(2,1)} copy(bf16[1280,5120]{0,1:T(8,128)(2,1)} %fusion.3) | data formatting | bytes 26214400 | tf_op jit(solution)/shard_map/convert_element_type | solution.py:41
  (4 shorter events, 0.0 us)
Async XLA Ops:
  6.5 79.1 %copy-start.2 = (s32[1,4]{1,0:T(1,128)S(1)}, s32[1,4]{1,0:T(1,128)}, u32[]{:S(2)}) copy-start(s32[1,4]{1,0:T(1,128)} %param.7) | copy-start | bytes 52
  6.5 79.2 %copy-start.3 = (f32[4]{0:T(128)S(1)}, f32[4]{0:T(128)}, u32[]{:S(2)}) copy-start(f32[4]{0:T(128)} %param.9) | copy-start | bytes 52
  6.5 79.2 %copy-start.4 = (s32[1,4]{1,0:T(1,128)S(1)}, s32[1,4]{1,0:T(1,128)}, u32[]{:S(2)}) copy-start(s32[1,4]{1,0:T(1,128)} %param.8) | copy-start | bytes 52
  6.5 68.9 %all-reduce.2.cloned.1.call-start = ((), (), s32[]{:S(2)}) async-start(), calls=%async_computation.1 | async-start | bytes 1310720 | tf_op jit(solution)/shard_map/psum | solution.py:20
  12.6 171.7 %all-gather.2.cloned.1.call-start = ((), (), s32[]{:S(2)}) async-start(), calls=%async_computation.2 | async-start | bytes 11141120 | tf_op jit(solution)/shard_map/all_gather | solution.py:21
  78.9 46.4 %all-to-all-start = ((bf16[64,16,1280]{2,0,1:T(8,128)(2,1)}), bf16[64,16,1280]{2,0,1:T(8,128)(2,1)S(1)}, u32[]{:S(2)}, u32[]{:S(2)}) async-start(bf16[64,16,1280]{2,0,1:T(8,128)(2,1)} %bitcast.28), calls=%async_computation | async-start | bytes 5242880 | tf_op jit(solution)/shard_map/all_to_all | solution.py:22
  125.3 1.5 copy-start.1
  184.3 7.0 %copy-start = (bf16[1024,5120]{1,0:T(8,128)(2,1)S(1)}, bf16[1024,5120]{1,0:T(8,128)(2,1)}, u32[]{:S(2)}) copy-start(bf16[1024,5120]{1,0:T(8,128)(2,1)} %all-gather.2.cloned.1.call-done) | copy-start | bytes 31457284
Sparse Core Ops, SparseCore 0:
  12.8 62.6 all-reduce.1
  77.5 106.7 all-gather.1
where the time goes:
time: 237 us; the launch traced here: 236 us
  waiting for transfers between devices  160 us (68%)
  local copies, waits for them, and re-layouts  25.1 us (11%)
  matrix products  20.5 us (9%)
  between operations  15.9 us (7%)
  other arithmetic  8.38 us (4%)
  starting transfers between devices  6.71 us (3%)
    psum x1, waiting for transfers between devices, per_device(): local_panels = lax.psum(jnp.concatenate(chunks, axis=1), 'row')  62.7 us
    all_gather x1, waiting for transfers between devices, per_device(): panels = lax.all_gather(local_panels, 'col', axis=0, tiled=True)  57.5 us
    all_to_all x1, waiting for transfers between devices, per_device(): lax.all_to_all(mock_maps, 'col', split_axis=1, concat_axis=0, tiled=True)  39.3 us
    dot_general x1, matrix products, per_device(): lax.dot_general(own_block, panels, (((0,), (0,)), ((), ())), preferred_el...  20.5 us
    convert_element_type x1, local copies, waits for them, and re-layouts, per_device(): return tile_value.astype(jnp.bfloat16)  17.6 us
    all_to_all x1, starting transfers between devices, per_device(): lax.all_to_all(mock_maps, 'col', split_axis=1, concat_axis=0, tiled=True)  6.66 us
    reduce_sum x1, other arithmetic, per_device(): panel_mean = jnp.sum(panels, axis=0, dtype=jnp.float32) / mock_count  5.61 us
  transfers between devices with their start and end apart: 3, of which 3 were waited for; matrix products, arithmetic and copies ran while one was open for 2% of the time, Pallas kernels for 0%

commit v1 on v0

--- a/solution.py
+++ b/solution.py
@@ -4,6 +4,19 @@
 from jax.sharding import PartitionSpec as P
 
 WINDOW = 4
+
+
+def ring_gather(x, axis, dim):
+    ways = lax.axis_size(axis)
+    up = [(d, (d + 1) % ways) for d in range(ways)]
+    down = [(d, (d - 1) % ways) for d in range(ways)]
+    earlier, later = ([x], [x])
+    for _ in range(ways // 2):
+        earlier.append(lax.ppermute(earlier[-1], axis, up))
+    for _ in range((ways - 1) // 2):
+        later.append(lax.ppermute(later[-1], axis, down))
+    line = jnp.concatenate([*earlier[::-1], *later[1:]], axis=dim)
+    return jnp.roll(line, (lax.axis_index(axis) - ways // 2) * x.shape[dim], axis=dim)
 
 
 def per_device(mock_maps, window_blocks, kept_tiles, taper_index, taper_table):
@@ -18,7 +31,7 @@
         piece = lax.dynamic_slice_in_dim(mock_maps, start, block_width, 1)
         chunks.append(jnp.where(mine, piece, jnp.zeros_like(piece)))
     local_panels = lax.psum(jnp.concatenate(chunks, axis=1), "row")
-    panels = lax.all_gather(local_panels, "col", axis=0, tiled=True)
+    panels = ring_gather(local_panels, "col", 0)
     own_block = lax.all_to_all(mock_maps, "col", split_axis=1, concat_axis=0, tiled=True)
     mock_count = own_block.shape[0]
     own_mean = jnp.sum(own_block, axis=0, dtype=jnp.float32) / mock_count

time: 237 us -> 359 us (1.51)
  the two profiles are of different devices: /device:TPU:1 before, /device:TPU:24 now
where the time goes in v1:
time: 359 us; the launch traced here: 357 us
  waiting for transfers between devices  183 us (51%)
  local copies, waits for them, and re-layouts  78.7 us (22%)
  starting transfers between devices  46.8 us (13%)
  matrix products  23.1 us (6%)
  between operations  16.2 us (5%)
  other arithmetic  9.55 us (3%)
    ppermute x8, waiting for transfers between devices, ring_gather(): earlier.append(lax.ppermute(earlier[-1], axis, up))  68.2 us
    psum x1, waiting for transfers between devices, per_device(): local_panels = lax.psum(jnp.concatenate(chunks, axis=1), 'row')  61.5 us
    unnamed x57, local copies, waits for them, and re-layouts  55.1 us
    ppermute x7, waiting for transfers between devices, ring_gather(): later.append(lax.ppermute(later[-1], axis, down))  53 us
    ppermute x7, starting transfers between devices, ring_gather(): later.append(lax.ppermute(later[-1], axis, down))  38.6 us
    dot_general x1, matrix products, per_device(): lax.dot_general(own_block, panels, (((0,), (0,)), ((), ())), preferred_el...  23.1 us
    convert_element_type x1, local copies, waits for them, and re-layouts, per_device(): return tile_value.astype(jnp.bfloat16)  17.6 us
  transfers between devices with their start and end apart: 17, of which 10 were waited for; matrix products, arithmetic and copies ran while one was open for 10% of the time, Pallas kernels for 0%

profile of v1, /device:TPU:24, one launch (start us, length us, event | category | flops | bytes accessed | tf_op | source)
XLA Modules:
  0.0 357.1 jit_solution(2691296639391711961)
XLA Ops:
  6.5 1.5 fusion.6
  10.6 1.3 dynamic-slice_select_fusion.3
  11.9 0.9 pad_maximum_fusion
  12.8 61.5 %all-reduce.2.cloned.1.call-done = bf16[64,5120]{1,0:T(8,128)(2,1)} async-done(((bf16[64,5120]{1,0:T(8,128)(2,1)}), bf16[64,5120]{1,0:T(8,128)(2,1)}) %all-reduce.2.cloned.1.call-update) | async-done | bytes 655376 | tf_op jit(solution)/shard_map/psum | solution.py:33
  74.3 1.5 collective-permute-start
  75.8 19.6 %collective-permute-done = bf16[64,5120]{1,0:T(8,128)(2,1)S(1)} collective-permute-done((bf16[64,5120]{1,0:T(8,128)(2,1)}, bf16[64,5120]{1,0:T(8,128)(2,1)S(1)}, u32[]{:S(2)}, u32[]{:S(2)}) %collective-permute-start) | collective-permute-done | bytes 655392 | tf_op jit(solution)/shard_map/ppermute | solution.py:15
  95.4 0.9 copy-done.1
  96.3 5.3 %collective-permute-start.8 = (bf16[64,5120]{1,0:T(8,128)(2,1)}, bf16[64,5120]{1,0:T(8,128)(2,1)}, u32[]{:S(2)}, u32[]{:S(2)}) collective-permute-start(bf16[64,5120]{1,0:T(8,128)(2,1)} %all-reduce.2.cloned.1.call-done), channel_id=1, source_target_pairs={{0,15},{1,0},{2,1},{3,2},{4,3},{5,4},{6,5},{7,6},{8,7},{9,8},{10,9... | collective-permute-start | bytes 1966088 | tf_op jit(solution)/shard_map/ppermute | solution.py:17
  101.6 14.7 %collective-permute-done.1 = bf16[64,5120]{1,0:T(8,128)(2,1)S(1)} collective-permute-done((bf16[64,5120]{1,0:T(8,128)(2,1)S(1)}, bf16[64,5120]{1,0:T(8,128)(2,1)S(1)}, u32[]{:S(2)}, u32[]{:S(2)}) %collective-permute-start.1) | collective-permute-done | bytes 655392 | tf_op jit(solution)/shard_map/ppermute | solution.py:15
  116.3 0.8 copy-done.3
  117.2 5.3 %collective-permute-start.9 = (bf16[64,5120]{1,0:T(8,128)(2,1)}, bf16[64,5120]{1,0:T(8,128)(2,1)}, u32[]{:S(2)}, u32[]{:S(2)}) collective-permute-start(bf16[64,5120]{1,0:T(8,128)(2,1)} %collective-permute-done.8), channel_id=1, source_target_pairs={{0,15},{1,0},{2,1},{3,2},{4,3},{5,4},{6,5},{7,6},{8,7},{9,8},{10,9... | collective-permute-start | bytes 1966088 | tf_op jit(solution)/shard_map/ppermute | solution.py:17
  122.5 13.9 %collective-permute-done.2 = bf16[64,5120]{1,0:T(8,128)(2,1)} collective-permute-done((bf16[64,5120]{1,0:T(8,128)(2,1)S(1)}, bf16[64,5120]{1,0:T(8,128)(2,1)}, u32[]{:S(2)}, u32[]{:S(2)}) %collective-permute-start.2) | collective-permute-done | bytes 655392 | tf_op jit(solution)/shard_map/ppermute | solution.py:15
  136.4 3.5 copy.16
  139.9 6.7 %all-to-all-start = ((bf16[64,16,1280]{2,0,1:T(8,128)(2,1)}), bf16[64,16,1280]{2,0,1:T(8,128)(2,1)S(1)}, u32[]{:S(2)}, u32[]{:S(2)}) async-start(bf16[64,16,1280]{2,0,1:T(8,128)(2,1)} %bitcast.27), calls=%async_computation | async-start | bytes 5242880 | tf_op jit(solution)/shard_map/all_to_all | solution.py:35
  146.7 5.3 %collective-permute-start.10 = (bf16[64,5120]{1,0:T(8,128)(2,1)}, bf16[64,5120]{1,0:T(8,128)(2,1)S(1)}, u32[]{:S(2)}, u32[]{:S(2)}) collective-permute-start(bf16[64,5120]{1,0:T(8,128)(2,1)} %collective-permute-done.9), channel_id=1, source_target_pairs={{0,15},{1,0},{2,1},{3,2},{4,3},{5,4},{6,5},{7,6},{8,7},{9,8},{10,9... | collective-permute-start | bytes 1966088 | tf_op jit(solution)/shard_map/ppermute | solution.py:17
  152.0 18.3 %collective-permute-done.3 = bf16[64,5120]{1,0:T(8,128)(2,1)} collective-permute-done((bf16[64,5120]{1,0:T(8,128)(2,1)}, bf16[64,5120]{1,0:T(8,128)(2,1)}, u32[]{:S(2)}, u32[]{:S(2)}) %collective-permute-start.3) | collective-permute-done | bytes 655392 | tf_op jit(solution)/shard_map/ppermute | solution.py:15
  170.3 20.3 %collective-permute-done.10 = bf16[64,5120]{1,0:T(8,128)(2,1)S(1)} collective-permute-done((bf16[64,5120]{1,0:T(8,128)(2,1)}, bf16[64,5120]{1,0:T(8,128)(2,1)S(1)}, u32[]{:S(2)}, u32[]{:S(2)}) %collective-permute-start.10) | collective-permute-done | bytes 655392 | tf_op jit(solution)/shard_map/ppermute | solution.py:17
  190.6 0.9 copy-done.5
  191.5 5.1 %collective-permute-start.11 = (bf16[64,5120]{1,0:T(8,128)(2,1)S(1)}, bf16[64,5120]{1,0:T(8,128)(2,1)S(1)}, u32[]{:S(2)}, u32[]{:S(2)}) collective-permute-start(bf16[64,5120]{1,0:T(8,128)(2,1)S(1)} %collective-permute-done.10), channel_id=1, source_target_pairs={{0,15},{1,0},{2,1},{3,2},{4,3},{5,4},{6,5},{7,6},{8,7},{9,8},{10,9... | collective-permute-start | bytes 1966088 | tf_op jit(solution)/shard_map/ppermute | solution.py:17
  196.6 1.7 collective-permute-done.4
  198.3 11.3 %collective-permute-done.11 = bf16[64,5120]{1,0:T(8,128)(2,1)S(1)} collective-permute-done((bf16[64,5120]{1,0:T(8,128)(2,1)S(1)}, bf16[64,5120]{1,0:T(8,128)(2,1)S(1)}, u32[]{:S(2)}, u32[]{:S(2)}) %collective-permute-start.11) | collective-permute-done | bytes 655392 | tf_op jit(solution)/shard_map/ppermute | solution.py:17
  209.6 0.8 copy-done.7
  210.4 5.8 %collective-permute-start.12 = (bf16[64,5120]{1,0:T(8,128)(2,1)S(1)}, bf16[64,5120]{1,0:T(8,128)(2,1)}, u32[]{:S(2)}, u32[]{:S(2)}) collective-permute-start(bf16[64,5120]{1,0:T(8,128)(2,1)S(1)} %collective-permute-done.11), channel_id=1, source_target_pairs={{0,15},{1,0},{2,1},{3,2},{4,3},{5,4},{6,5},{7,6},{8,7},{9,8},{10,9... | collective-permute-start | bytes 1966088 | tf_op jit(solution)/shard_map/ppermute | solution.py:17
  216.3 12.1 %collective-permute-done.12 = bf16[64,5120]{1,0:T(8,128)(2,1)} collective-permute-done((bf16[64,5120]{1,0:T(8,128)(2,1)S(1)}, bf16[64,5120]{1,0:T(8,128)(2,1)}, u32[]{:S(2)}, u32[]{:S(2)}) %collective-permute-start.12) | collective-permute-done | bytes 655392 | tf_op jit(solution)/shard_map/ppermute | solution.py:17
  228.4 5.9 %collective-permute-start.13 = (bf16[64,5120]{1,0:T(8,128)(2,1)}, bf16[64,5120]{1,0:T(8,128)(2,1)}, u32[]{:S(2)}, u32[]{:S(2)}) collective-permute-start(bf16[64,5120]{1,0:T(8,128)(2,1)} %collective-permute-done.12), channel_id=1, source_target_pairs={{0,15},{1,0},{2,1},{3,2},{4,3},{5,4},{6,5},{7,6},{8,7},{9,8},{10,9... | collective-permute-start | bytes 1966088 | tf_op jit(solution)/shard_map/ppermute | solution.py:17
  234.3 0.9 select_reduce_fusion
  235.3 0.7 compare_bitcast_fusion
  236.5 9.3 %collective-permute-done.13 = bf16[64,5120]{1,0:T(8,128)(2,1)} collective-permute-done((bf16[64,5120]{1,0:T(8,128)(2,1)}, bf16[64,5120]{1,0:T(8,128)(2,1)}, u32[]{:S(2)}, u32[]{:S(2)}) %collective-permute-start.13) | collective-permute-done | bytes 655392 | tf_op jit(solution)/shard_map/ppermute | solution.py:17
  245.9 5.8 %collective-permute-start.14 = (bf16[64,5120]{1,0:T(8,128)(2,1)}, bf16[64,5120]{1,0:T(8,128)(2,1)S(1)}, u32[]{:S(2)}, u32[]{:S(2)}) collective-permute-start(bf16[64,5120]{1,0:T(8,128)(2,1)} %collective-permute-done.13), channel_id=1, source_target_pairs={{0,15},{1,0},{2,1},{3,2},{4,3},{5,4},{6,5},{7,6},{8,7},{9,8},{10,9... | collective-permute-start | bytes 1966088 | tf_op jit(solution)/shard_map/ppermute | solution.py:17
  251.7 2.0 constant_dynamic-update-slice_fusion.31
  253.7 2.0 constant_dynamic-update-slice_fusion.30
  255.6 2.0 constant_dynamic-update-slice_fusion.29
  257.6 2.0 constant_dynamic-update-slice_fusion.28
  259.6 2.0 constant_dynamic-update-slice_fusion.27
  261.5 2.0 constant_dynamic-update-slice_fusion.26
  263.5 2.0 constant_dynamic-update-slice_fusion.25
  265.5 2.0 constant_dynamic-update-slice_fusion.24
  267.5 0.9 constant_dynamic-update-slice_fusion.23
  268.4 2.0 constant_dynamic-update-slice_fusion.22
  270.3 2.0 constant_dynamic-update-slice_fusion.21
  272.3 2.0 constant_dynamic-update-slice_fusion.20
  274.3 2.0 constant_dynamic-update-slice_fusion.19
  276.3 2.0 constant_dynamic-update-slice_fusion.18
  278.3 2.0 constant_dynamic-update-slice_fusion.17
  280.3 0.9 constant_dynamic-update-slice_fusion.16
  281.2 2.0 constant_dynamic-update-slice_fusion.15
  283.2 2.0 constant_dynamic-update-slice_fusion.14
  285.2 0.9 constant_dynamic-update-slice_fusion.13
  286.1 0.9 constant_dynamic-update-slice_fusion.12
  287.0 2.0 constant_dynamic-update-slice_fusion.11
  289.0 2.0 constant_dynamic-update-slice_fusion.10
  290.9 0.9 constant_dynamic-update-slice_fusion.9
  291.8 0.9 constant_dynamic-update-slice_fusion.8
  292.7 0.9 constant_dynamic-update-slice_fusion.7
  293.6 2.0 constant_dynamic-update-slice_fusion.6
  295.6 2.0 constant_dynamic-update-slice_fusion.5
  297.6 0.9 constant_dynamic-update-slice_fusion.4
  298.5 0.9 constant_dynamic-update-slice_fusion.3
  299.3 2.0 constant_dynamic-update-slice_fusion.2
  301.3 2.0 constant_dynamic-update-slice_fusion.1
  303.3 0.9 constant_dynamic-update-slice_fusion
  304.2 5.4 %convert_reduce_fusion = f32[5120]{0:T(1024)S(1)} fusion(bf16[2048,5120]{1,0:T(8,128)(2,1)} %constant_dynamic-update-slice_fusion, s32[]{:T(128)S(6)} %select_n.73), kind=kLoop, calls=%fused_computation.5 | loop fusion | flops 10480640 | bytes 10506244 | tf_op jit(solution)/shard_map/reduce_sum | solution.py:38
  309.6 23.1 %fusion.3 = bf16[1280,5120]{0,1:T(8,128)(2,1)} fusion(bf16[1024,1280]{1,0:T(8,128)(2,1)S(1)} %bitcast.26, f32[5120]{0:T(1024)S(1)} %broadcast_multiply_fusion, f32[1280]{0:T(1024)S(1)} %convert_reduce_fusion.1, f32[5120]{0:T(1024)S(1)} %mul.48, pred[5120]{0:T(1024)(128)(4,1)S(1)} %gt.21, bf16[2048,5120]{1,0:T(8,128)(2,1)} %constant_dynamic-update-slice_fusion, ...), kind=kOutput, calls=%fused_computation.4 | convolution fusion | flops 13461094400 | bytes 26265604 | tf_op jit(solution)/shard_map/dot_general | solution.py:39
  332.7 17.6 %copy.13 = bf16[1280,5120]{1,0:T(8,128)(2,1)} copy(bf16[1280,5120]{0,1:T(8,128)(2,1)} %fusion.3) | data formatting | bytes 26214400 | tf_op jit(solution)/shard_map/convert_element_type | solution.py:54
  (44 shorter events, 0.7 us)
Async XLA Ops:
  6.5 67.8 %all-reduce.2.cloned.1.call-start = ((), (), s32[]{:S(2)}) async-start(), calls=%async_computation.1 | async-start | bytes 1310720 | tf_op jit(solution)/shard_map/psum | solution.py:33
  74.3 193.1 %copy-start = (bf16[64,5120]{1,0:T(8,128)(2,1)S(1)}, bf16[64,5120]{1,0:T(8,128)(2,1)}, u32[]{:S(2)}) copy-start(bf16[64,5120]{1,0:T(8,128)(2,1)} %all-reduce.2.cloned.1.call-done) | copy-start | bytes 1966084
  74.3 21.1 %collective-permute-start = (bf16[64,5120]{1,0:T(8,128)(2,1)}, bf16[64,5120]{1,0:T(8,128)(2,1)S(1)}, u32[]{:S(2)}, u32[]{:S(2)}) collective-permute-start(bf16[64,5120]{1,0:T(8,128)(2,1)} %all-reduce.2.cloned.1.call-done), channel_id=1, source_target_pairs={{0,1},{1,2},{2,3},{3,4},{4,5},{5,6},{6,7},{7,8},{8,9},{9,10},{10,1... | collective-permute-start | bytes 1966088 | tf_op jit(solution)/shard_map/ppermute | solution.py:15
  95.4 0.9 copy-start.1
  96.3 20.0 %collective-permute-start.1 = (bf16[64,5120]{1,0:T(8,128)(2,1)S(1)}, bf16[64,5120]{1,0:T(8,128)(2,1)S(1)}, u32[]{:S(2)}, u32[]{:S(2)}) collective-permute-start(bf16[64,5120]{1,0:T(8,128)(2,1)S(1)} %collective-permute-done), channel_id=1, source_target_pairs={{0,1},{1,2},{2,3},{3,4},{4,5},{5,6},{6,7},{7,8},{8,9},{9,10},{10,1... | collective-permute-start | bytes 1966088 | tf_op jit(solution)/shard_map/ppermute | solution.py:15
  96.3 20.9 %collective-permute-start.8 = (bf16[64,5120]{1,0:T(8,128)(2,1)}, bf16[64,5120]{1,0:T(8,128)(2,1)}, u32[]{:S(2)}, u32[]{:S(2)}) collective-permute-start(bf16[64,5120]{1,0:T(8,128)(2,1)} %all-reduce.2.cloned.1.call-done), channel_id=1, source_target_pairs={{0,15},{1,0},{2,1},{3,2},{4,3},{5,4},{6,5},{7,6},{8,7},{9,8},{10,9... | collective-permute-start | bytes 1966088 | tf_op jit(solution)/shard_map/ppermute | solution.py:17
  116.3 0.9 copy-start.3
  117.2 19.3 %collective-permute-start.2 = (bf16[64,5120]{1,0:T(8,128)(2,1)S(1)}, bf16[64,5120]{1,0:T(8,128)(2,1)}, u32[]{:S(2)}, u32[]{:S(2)}) collective-permute-start(bf16[64,5120]{1,0:T(8,128)(2,1)S(1)} %collective-permute-done.1), channel_id=1, source_target_pairs={{0,1},{1,2},{2,3},{3,4},{4,5},{5,6},{6,7},{7,8},{8,9},{9,10},{10,1... | collective-permute-start | bytes 1966088 | tf_op jit(solution)/shard_map/ppermute | solution.py:15
  117.2 29.5 %collective-permute-start.9 = (bf16[64,5120]{1,0:T(8,128)(2,1)}, bf16[64,5120]{1,0:T(8,128)(2,1)}, u32[]{:S(2)}, u32[]{:S(2)}) collective-permute-start(bf16[64,5120]{1,0:T(8,128)(2,1)} %collective-permute-done.8), channel_id=1, source_target_pairs={{0,15},{1,0},{2,1},{3,2},{4,3},{5,4},{6,5},{7,6},{8,7},{9,8},{10,9... | collective-permute-start | bytes 1966088 | tf_op jit(solution)/shard_map/ppermute | solution.py:17
  136.4 33.9 %collective-permute-start.3 = (bf16[64,5120]{1,0:T(8,128)(2,1)}, bf16[64,5120]{1,0:T(8,128)(2,1)}, u32[]{:S(2)}, u32[]{:S(2)}) collective-permute-start(bf16[64,5120]{1,0:T(8,128)(2,1)} %collective-permute-done.2), channel_id=1, source_target_pairs={{0,1},{1,2},{2,3},{3,4},{4,5},{5,6},{6,7},{7,8},{8,9},{9,10},{10,1... | collective-permute-start | bytes 1966088 | tf_op jit(solution)/shard_map/ppermute | solution.py:15
  139.9 96.1 %all-to-all-start = ((bf16[64,16,1280]{2,0,1:T(8,128)(2,1)}), bf16[64,16,1280]{2,0,1:T(8,128)(2,1)S(1)}, u32[]{:S(2)}, u32[]{:S(2)}) async-start(bf16[64,16,1280]{2,0,1:T(8,128)(2,1)} %bitcast.27), calls=%async_computation | async-start | bytes 5242880 | tf_op jit(solution)/shard_map/all_to_all | solution.py:35
  146.7 44.0 %collective-permute-start.10 = (bf16[64,5120]{1,0:T(8,128)(2,1)}, bf16[64,5120]{1,0:T(8,128)(2,1)S(1)}, u32[]{:S(2)}, u32[]{:S(2)}) collective-permute-start(bf16[64,5120]{1,0:T(8,128)(2,1)} %collective-permute-done.9), channel_id=1, source_target_pairs={{0,15},{1,0},{2,1},{3,2},{4,3},{5,4},{6,5},{7,6},{8,7},{9,8},{10,9... | collective-permute-start | bytes 1966088 | tf_op jit(solution)/shard_map/ppermute | solution.py:17
  170.3 28.0 %collective-permute-start.4 = (bf16[64,5120]{1,0:T(8,128)(2,1)}, bf16[64,5120]{1,0:T(8,128)(2,1)S(1)}, u32[]{:S(2)}, u32[]{:S(2)}) collective-permute-start(bf16[64,5120]{1,0:T(8,128)(2,1)} %collective-permute-done.3), channel_id=1, source_target_pairs={{0,1},{1,2},{2,3},{3,4},{4,5},{5,6},{6,7},{7,8},{8,9},{9,10},{10,1... | collective-permute-start | bytes 1966088 | tf_op jit(solution)/shard_map/ppermute | solution.py:15
  190.6 0.9 copy-start.5
  191.5 18.1 %collective-permute-start.11 = (bf16[64,5120]{1,0:T(8,128)(2,1)S(1)}, bf16[64,5120]{1,0:T(8,128)(2,1)S(1)}, u32[]{:S(2)}, u32[]{:S(2)}) collective-permute-start(bf16[64,5120]{1,0:T(8,128)(2,1)S(1)} %collective-permute-done.10), channel_id=1, source_target_pairs={{0,15},{1,0},{2,1},{3,2},{4,3},{5,4},{6,5},{7,6},{8,7},{9,8},{10,9... | collective-permute-start | bytes 1966088 | tf_op jit(solution)/shard_map/ppermute | solution.py:17
  198.3 30.0 %copy-start.9 = (bf16[64,5120]{1,0:T(8,128)(2,1)}, bf16[64,5120]{1,0:T(8,128)(2,1)S(1)}, u32[]{:S(2)}) copy-start(bf16[64,5120]{1,0:T(8,128)(2,1)S(1)} %collective-permute-done.4) | copy-start | bytes 1966084
  198.3 17.9 %collective-permute-start.5 = (bf16[64,5120]{1,0:T(8,128)(2,1)S(1)}, bf16[64,5120]{1,0:T(8,128)(2,1)S(1)}, u32[]{:S(2)}, u32[]{:S(2)}) collective-permute-start(bf16[64,5120]{1,0:T(8,128)(2,1)S(1)} %collective-permute-done.4), channel_id=1, source_target_pairs={{0,1},{1,2},{2,3},{3,4},{4,5},{5,6},{6,7},{7,8},{8,9},{9,10},{10,1... | collective-permute-start | bytes 1966088 | tf_op jit(solution)/shard_map/ppermute | solution.py:15
  209.6 0.8 copy-start.7
  210.4 17.9 %collective-permute-start.12 = (bf16[64,5120]{1,0:T(8,128)(2,1)S(1)}, bf16[64,5120]{1,0:T(8,128)(2,1)}, u32[]{:S(2)}, u32[]{:S(2)}) collective-permute-start(bf16[64,5120]{1,0:T(8,128)(2,1)S(1)} %collective-permute-done.11), channel_id=1, source_target_pairs={{0,15},{1,0},{2,1},{3,2},{4,3},{5,4},{6,5},{7,6},{8,7},{9,8},{10,9... | collective-permute-start | bytes 1966088 | tf_op jit(solution)/shard_map/ppermute | solution.py:17
  216.3 18.0 %copy-start.11 = (bf16[64,5120]{1,0:T(8,128)(2,1)}, bf16[64,5120]{1,0:T(8,128)(2,1)S(1)}, u32[]{:S(2)}) copy-start(bf16[64,5120]{1,0:T(8,128)(2,1)S(1)} %collective-permute-done.5) | copy-start | bytes 1966084
  216.3 18.0 %collective-permute-start.6 = (bf16[64,5120]{1,0:T(8,128)(2,1)S(1)}, bf16[64,5120]{1,0:T(8,128)(2,1)}, u32[]{:S(2)}, u32[]{:S(2)}) collective-permute-start(bf16[64,5120]{1,0:T(8,128)(2,1)S(1)} %collective-permute-done.5), channel_id=1, source_target_pairs={{0,1},{1,2},{2,3},{3,4},{4,5},{5,6},{6,7},{7,8},{8,9},{9,10},{10,1... | collective-permute-start | bytes 1966088 | tf_op jit(solution)/shard_map/ppermute | solution.py:15
  228.4 17.5 %collective-permute-start.13 = (bf16[64,5120]{1,0:T(8,128)(2,1)}, bf16[64,5120]{1,0:T(8,128)(2,1)}, u32[]{:S(2)}, u32[]{:S(2)}) collective-permute-start(bf16[64,5120]{1,0:T(8,128)(2,1)} %collective-permute-done.12), channel_id=1, source_target_pairs={{0,15},{1,0},{2,1},{3,2},{4,3},{5,4},{6,5},{7,6},{8,7},{9,8},{10,9... | collective-permute-start | bytes 1966088 | tf_op jit(solution)/shard_map/ppermute | solution.py:17
  234.3 17.4 %collective-permute-start.7 = (bf16[64,5120]{1,0:T(8,128)(2,1)}, bf16[64,5120]{1,0:T(8,128)(2,1)}, u32[]{:S(2)}, u32[]{:S(2)}) collective-permute-start(bf16[64,5120]{1,0:T(8,128)(2,1)} %collective-permute-done.6), channel_id=1, source_target_pairs={{0,1},{1,2},{2,3},{3,4},{4,5},{5,6},{6,7},{7,8},{8,9},{9,10},{10,1... | collective-permute-start | bytes 1966088 | tf_op jit(solution)/shard_map/ppermute | solution.py:15
  236.0 49.1 %copy-start.12 = (bf16[64,5120]{1,0:T(8,128)(2,1)S(1)}, bf16[64,5120]{1,0:T(8,128)(2,1)}, u32[]{:S(2)}) copy-start(bf16[64,5120]{1,0:T(8,128)(2,1)} %copy-done.11) | copy-start | bytes 1966084
  236.0 50.0 %copy-start.10 = (bf16[64,5120]{1,0:T(8,128)(2,1)S(1)}, bf16[64,5120]{1,0:T(8,128)(2,1)}, u32[]{:S(2)}) copy-start(bf16[64,5120]{1,0:T(8,128)(2,1)} %copy-done.9) | copy-start | bytes 1966084
  236.0 54.9 %copy-start.4 = (bf16[64,5120]{1,0:T(8,128)(2,1)S(1)}, bf16[64,5120]{1,0:T(8,128)(2,1)}, u32[]{:S(2)}) copy-start(bf16[64,5120]{1,0:T(8,128)(2,1)} %copy-done.3) | copy-start | bytes 1966084
  236.1 55.7 %copy-start.2 = (bf16[64,5120]{1,0:T(8,128)(2,1)S(1)}, bf16[64,5120]{1,0:T(8,128)(2,1)}, u32[]{:S(2)}) copy-start(bf16[64,5120]{1,0:T(8,128)(2,1)} %copy-done.1) | copy-start | bytes 1966084
  236.1 61.5 %copy-start.6 = (bf16[64,5120]{1,0:T(8,128)(2,1)S(1)}, bf16[64,5120]{1,0:T(8,128)(2,1)}, u32[]{:S(2)}) copy-start(bf16[64,5120]{1,0:T(8,128)(2,1)} %copy-done.5) | copy-start | bytes 1966084
  236.1 62.4 %copy-start.8 = (bf16[64,5120]{1,0:T(8,128)(2,1)S(1)}, bf16[64,5120]{1,0:T(8,128)(2,1)}, u32[]{:S(2)}) copy-start(bf16[64,5120]{1,0:T(8,128)(2,1)} %copy-done.7) | copy-start | bytes 1966084
  245.9 34.5 %collective-permute-start.14 = (bf16[64,5120]{1,0:T(8,128)(2,1)}, bf16[64,5120]{1,0:T(8,128)(2,1)S(1)}, u32[]{:S(2)}, u32[]{:S(2)}) collective-permute-start(bf16[64,5120]{1,0:T(8,128)(2,1)} %collective-permute-done.13), channel_id=1, source_target_pairs={{0,15},{1,0},{2,1},{3,2},{4,3},{5,4},{6,5},{7,6},{8,7},{9,8},{10,9... | collective-permute-start | bytes 1966088 | tf_op jit(solution)/shard_map/ppermute | solution.py:17
Sparse Core Ops, SparseCore 0:
  13.0 61.3 all-reduce.1
